TPU v7x, 512 devices: a whole 4x4x16 slice. The times are simulated.
512 devices in a mesh: row: 64 (over z, x), rep: 8 (over y, core).
Axes of the slice: x: 4, y: 4, z: 16, core: 2. Of those that a mesh axis runs over, the one named last changes fastest.
Arguments:
- features: bfloat16 [16384, 128], P('row', 'rep'), may hold values from -6 to 6
- owner_index: int32 [16384], P('row'), may hold values from 0 to 16383, as said below
- block_cols: int32 [128, 64], P('row', 'rep'), may hold values from 0 to 127, as said below
- block_count: int32 [128], P('row'), may hold values from 1 to 64, as said below
- tiles: bfloat16 [128, 64, 128, 128], P('row', 'rep'), may hold values from -0.109375 to 0.109375
- weight: bfloat16 [128, 256], P(None, 'rep'), may hold values from -0.75 to 0.75
- bias: float32 [256], P('rep'), may hold values from -4 to 4
- grad_out: bfloat16 [16384, 256], P('row', 'rep'), may hold values from -6 to 6
Outputs:
- hidden: bfloat16 [16384, 256], P('row', 'rep')
- weight_grad: float32 [128, 256], P(None, 'rep')
- bias_grad: float32 [256], P('rep')
Inputs may be any that keep to these rules, and one draw needn't show every extreme that they name: `owner_index`: A permutation; the 256 rows of each loader shard hold exactly 4 positions of every partition's 2*128 rows. `block_cols`: the block columns of one block row are distinct. Block column c belongs to partition c // 2. Over all slots of one partition's 2 block rows, exactly 1 distinct block columns of each partition are named. `block_count`: some block row has all 64 slots live.
All inputs are finite; a program needn't handle non-finite values.
Results may differ from a plain program's by a relative error of at most 0.017.
Values may be sent and summed in bfloat16 or wider, within the bound.
No kernel may reach another device: no remote copies, remote signals or barrier semaphores. Data moves between devices by JAX's collectives and lax.ppermute only.
A program may use at most 64 MiB of HBM per device.

v0:
```python
import jax
import jax.numpy as jnp
from jax import lax
from jax.sharding import PartitionSpec as P


def block_product(tile_set, col_set, live, table, rows_part):
    size_blk = tile_set.shape[2]
    width = table.shape[1]
    blocks = table.reshape(table.shape[0] // size_blk, size_blk, width)
    picked = blocks[col_set]
    picked = jnp.where(live[:, :, None, None], picked, jnp.zeros_like(picked))
    summed = jnp.einsum("rkij,rkjc->ric", tile_set, picked, preferred_element_type=jnp.float32)
    return summed.reshape(rows_part, width)


def on_device(features, owner_index, block_cols, block_count, tiles, weight, bias, grad_out):
    rows_part = features.shape[0]
    cols_dev = features.shape[1]
    parts_count = lax.axis_size("row")
    per_pair = rows_part // parts_count
    destination = owner_index // rows_part
    order = jnp.argsort(destination, stable=True)
    send_rows = features[order].reshape(parts_count, per_pair, cols_dev)
    send_pos = (owner_index[order] % rows_part).reshape(parts_count, per_pair)
    got_rows, got_pos = (
        lax.all_to_all(send_rows, "row", split_axis=0, concat_axis=0, tiled=True),
        lax.all_to_all(send_pos, "row", split_axis=0, concat_axis=0, tiled=True),
    )
    owned = (
        jnp.zeros((rows_part, cols_dev), jnp.bfloat16)
        .at[got_pos.reshape(rows_part)]
        .set(got_rows.reshape(rows_part, cols_dev))
    )
    wide_own = lax.all_gather(owned, "rep", axis=1, tiled=True)
    table = lax.all_gather(wide_own, "row", axis=0, tiled=True)
    slots_dev = block_cols.shape[1]
    slot_ids = lax.axis_index("rep") * slots_dev + jnp.arange(slots_dev, dtype=jnp.int32)
    live = slot_ids[None, :] < block_count[:, None]
    partial_agg = block_product(tiles, block_cols, live, table, rows_part)
    agg = lax.psum(partial_agg.astype(jnp.bfloat16), "rep")
    pre = jnp.dot(agg, weight, preferred_element_type=jnp.float32) + bias
    hidden = jax.nn.silu(pre).astype(jnp.bfloat16)
    sig = jax.nn.sigmoid(pre)
    dpre = (grad_out.astype(jnp.float32) * sig * (1.0 + pre * (1.0 - sig))).astype(jnp.bfloat16)
    weight_term = jnp.dot(agg.T, dpre, preferred_element_type=jnp.float32)
    bias_term = jnp.sum(dpre.astype(jnp.float32), axis=0)
    weight_grad, bias_grad = lax.psum((weight_term, bias_term), "row")
    return (hidden, weight_grad, bias_grad)


def solution(mesh):
    placed = (
        P("row", "rep"),
        P("row"),
        P("row", "rep"),
        P("row"),
        P("row", "rep", None, None),
        P(None, "rep"),
        P("rep"),
        P("row", "rep"),
    )
    return jax.shard_map(
        on_device,
        mesh=mesh,
        in_specs=placed,
        out_specs=(P("row", "rep"), P(None, "rep"), P("rep")),
        check_vma=False,
    )
```

profile of v0, /device:TPU:8, one launch (start us, length us, event | category | flops | bytes accessed | tf_op | source)
XLA Modules:
  0.0 583.7 jit_solution(2200357898452502559)
XLA Ops:
  7.2 0.7 and_select_fusion
  7.9 3.2 sort.17
  11.1 2.0 gather_fusion
  13.2 0.6 add_select_fusion
  13.8 18.6 %all-to-all-start = ((s32[64,1,4]{2,1,0:T(1,128)}), s32[64,1,4]{2,1,0:T(1,128)S(1)}, u32[]{:S(2)}, u32[]{:S(2)}) async-start(s32[64,1,4]{2,1,0:T(1,128)} %bitcast), calls=%async_computation | async-start | bytes 65536 | tf_op jit(solution)/shard_map/all_to_all | solution.py:28
  32.4 0.8 copy.18
  33.2 1.5 gather_fusion.1
  34.7 12.5 %all-to-all-done = s32[64,1,4]{2,1,0:T(1,128)S(1)} async-done(((s32[64,1,4]{2,1,0:T(1,128)}), s32[64,1,4]{2,1,0:T(1,128)S(1)}, u32[]{:S(2)}, u32[]{:S(2)}) %all-to-all-start) | async-done | bytes 1056 | tf_op jit(solution)/shard_map/all_to_all | solution.py:28
  47.2 4.6 all-to-all-start.1
  51.8 0.5 broadcast.122
  52.3 0.7 reduce.3
  53.2 13.9 %all-to-all-done.1 = bf16[64,4,16]{2,1,0:T(4,128)(2,1)S(1)} async-done(((bf16[64,4,16]{2,1,0:T(4,128)(2,1)}), bf16[64,4,16]{2,1,0:T(4,128)(2,1)S(1)}, u32[]{:S(2)}, u32[]{:S(2)}) %all-to-all-start.1) | async-done | bytes 8224 | tf_op jit(solution)/shard_map/all_to_all | solution.py:27
  67.1 1.2 scatter_custom_fusion
  68.3 14.0 %all_gather.6 = bf16[256,128]{0,1:T(8,128)(2,1)} all-gather(bf16[256,16]{0,1:T(8,128)(2,1)S(1)} %copy.19), channel_id=1, replica_groups=mesh['row'=64,'rep'=8] {'rep'}, dimensions={1}, use_global_device_ids=true | all-gather | bytes 73728 | tf_op jit(solution)/shard_map/all_gather | solution.py:35
  82.4 0.7 compare_select_fusion.1
  83.2 0.7 broadcast_compare_fusion
  83.9 133.4 %all-gather.2.cloned.1.call-done = bf16[16384,128]{0,1:T(8,128)(2,1)} async-done(((bf16[256,128]{0,1:T(8,128)(2,1)}), bf16[16384,128]{0,1:T(8,128)(2,1)}) %all-gather.2.cloned.1.call-update) | async-done | bytes 4194320 | tf_op jit(solution)/shard_map/all_gather | solution.py:36
  217.4 6.4 %copy.20 = bf16[16384,128]{1,0:T(8,128)(2,1)} copy(bf16[16384,128]{0,1:T(8,128)(2,1)} %all-gather.2.cloned.1.call-done) | data formatting | bytes 8388608 | tf_op jit(solution)/shard_map/all_gather | solution.py:36
  223.7 2.8 gather_fusion.2
  226.6 1.0 fusion
  227.6 66.4 %all-reduce.3.cloned.1.call-done = bf16[256,128]{1,0:T(8,128)(2,1)} async-done(((bf16[256,128]{1,0:T(8,128)(2,1)}), bf16[256,128]{1,0:T(8,128)(2,1)}) %all-reduce.3.cloned.1.call-update) | async-done | bytes 65552 | tf_op jit(solution)/shard_map/psum | solution.py:41
  294.0 1.7 convert_reduce_fusion
  295.8 1.0 fusion.8
  296.7 280.1 %all-reduce = (f32[128,32]{0,1:T(8,128)}, f32[32]{0:T(128)}) all-reduce(f32[128,32]{0,1:T(8,128)S(1)} %fusion.8, f32[32]{0:T(128)S(1)} %get-tuple-element.7), channel_id=1, replica_groups=mesh['row'=64,'rep'=8] {'row'}, use_global_device_ids=true, to_apply=%region_3.4 | all-reduce | flops 4128 | bytes 33024 | tf_op jit(solution)/shard_map/psum | solution.py:48
  (22 shorter events, 0.5 us)
Async XLA Ops:
  7.2 219.4 %copy-start = (bf16[2,8,128,128]{3,2,1,0:T(8,128)(2,1)S(1)}, bf16[2,8,128,128]{3,2,1,0:T(8,128)(2,1)}, u32[]{:S(2)}) copy-start(bf16[2,8,128,128]{3,2,1,0:T(8,128)(2,1)} %param.12) | copy-start | bytes 1572868
  13.8 33.3 %all-to-all-start = ((s32[64,1,4]{2,1,0:T(1,128)}), s32[64,1,4]{2,1,0:T(1,128)S(1)}, u32[]{:S(2)}, u32[]{:S(2)}) async-start(s32[64,1,4]{2,1,0:T(1,128)} %bitcast), calls=%async_computation | async-start | bytes 65536 | tf_op jit(solution)/shard_map/all_to_all | solution.py:28
  47.2 19.9 %all-to-all-start.1 = ((bf16[64,4,16]{2,1,0:T(4,128)(2,1)}), bf16[64,4,16]{2,1,0:T(4,128)(2,1)S(1)}, u32[]{:S(2)}, u32[]{:S(2)}) async-start(bf16[64,4,16]{2,1,0:T(4,128)(2,1)} %bitcast.2), calls=%async_computation.1 | async-start | bytes 131072 | tf_op jit(solution)/shard_map/all_to_all | solution.py:27
  51.8 165.6 %all-gather.2.cloned.1.call-start = ((), (), s32[]{:S(2)}) async-start(), calls=%async_computation.2 | async-start | bytes 4259840 | tf_op jit(solution)/shard_map/all_gather | solution.py:36
  82.4 211.7 %all-reduce.3.cloned.1.call-start = ((), (), s32[]{:S(2)}) async-start(), calls=%async_computation.3 | async-start | bytes 131072 | tf_op jit(solution)/shard_map/psum | solution.py:41
  83.9 210.1 %copy-start.1 = (bf16[256,32]{0,1:T(8,128)(2,1)S(1)}, bf16[256,32]{0,1:T(8,128)(2,1)}, u32[]{:S(2)}) copy-start(bf16[256,32]{0,1:T(8,128)(2,1)} %param.15) | copy-start | bytes 49156
  83.9 210.1 %copy-start.2 = (bf16[128,32]{0,1:T(8,128)(2,1)S(1)}, bf16[128,32]{0,1:T(8,128)(2,1)}, u32[]{:S(2)}) copy-start(bf16[128,32]{0,1:T(8,128)(2,1)} %param.13) | copy-start | bytes 24580
  83.9 210.1 %copy-start.3 = (f32[32]{0:T(128)S(1)}, f32[32]{0:T(128)}, u32[]{:S(2)}) copy-start(f32[32]{0:T(128)} %param.14) | copy-start | bytes 388
Sparse Core Ops, SparseCore 0:
  82.5 134.8 all-gather.1
  227.7 66.2 all-reduce.2
where the time goes:
time: 584 us
  blocking collectives  294 us (50%)
  waiting for transfers between devices  226 us (39%)
  starting transfers between devices  23.3 us (4%)
  local copies, waits for them, and re-layouts  15.5 us (3%)
  between operations  14.1 us (2%)
  other arithmetic  6.69 us (1%)
    psum x1, blocking collectives, on_device(): weight_grad, bias_grad = lax.psum((weight_term, bias_term), 'row')  280 us
    all_gather x1, waiting for transfers between devices, on_device(): table = lax.all_gather(wide_own, 'row', axis=0, tiled=True)  133 us
    psum x1, waiting for transfers between devices, on_device(): agg = lax.psum(partial_agg.astype(jnp.bfloat16), 'rep')  66.4 us
    all_to_all x1, starting transfers between devices, on_device(): lax.all_to_all(send_pos, 'row', split_axis=0, concat_axis=0, tiled=True)  18.6 us
    all_gather x1, blocking collectives, on_device(): wide_own = lax.all_gather(owned, 'rep', axis=1, tiled=True)  14 us
    all_to_all x1, waiting for transfers between devices, on_device(): lax.all_to_all(send_rows, 'row', split_axis=0, concat_axis=0, tiled=True)  13.9 us
    all_to_all x1, waiting for transfers between devices, on_device(): lax.all_to_all(send_pos, 'row', split_axis=0, concat_axis=0, tiled=True)  12.5 us
  transfers between devices with their start and end apart: 4, of which 4 were waited for; matrix products, arithmetic and copies ran while one was open for 1% of the time, Pallas kernels for 0%

commit v1 on v0

--- a/solution.py
+++ b/solution.py
@@ -2,6 +2,28 @@
 import jax.numpy as jnp
 from jax import lax
 from jax.sharding import PartitionSpec as P
+
+
+def laid_out(blocks, dim):
+    shape = list(blocks.shape[1:])
+    shape[dim] *= blocks.shape[0]
+    return jnp.moveaxis(blocks, 0, dim).reshape(shape)
+
+
+def collect(value, axis, dim):
+    peers = lax.axis_size(axis)
+    pairs = [(i, (i + 1) % peers) for i in range(peers)]
+    back = [(b, a) for a, b in pairs]
+    lower, upper = ([], [])
+    for lap in range(peers - 1):
+        if lap % 2 == 0:
+            lower.append(lax.ppermute(lower[-1] if lower else value, axis, pairs))
+        else:
+            upper.append(lax.ppermute(upper[-1] if upper else value, axis, back))
+    blocks = jnp.stack([*lower[::-1], value, *upper])
+    shift = lax.axis_index(axis) - len(lower)
+    blocks = blocks[(jnp.arange(peers) - shift) % peers]
+    return laid_out(blocks, dim)
 
 
 def block_product(tile_set, col_set, live, table, rows_part):
@@ -32,7 +54,7 @@
         .at[got_pos.reshape(rows_part)]
         .set(got_rows.reshape(rows_part, cols_dev))
     )
-    wide_own = lax.all_gather(owned, "rep", axis=1, tiled=True)
+    wide_own = collect(owned, "rep", 1)
     table = lax.all_gather(wide_own, "row", axis=0, tiled=True)
     slots_dev = block_cols.shape[1]
     slot_ids = lax.axis_index("rep") * slots_dev + jnp.arange(slots_dev, dtype=jnp.int32)

time: 584 us -> 589 us (level)
  blocking collectives: 294 us -> 280 us
  waiting for transfers between devices: 226 us -> 238 us
    all_gather x1 -> x0, blocking collectives: 14 us -> none  [on_device(): wide_own = lax.all_gather(owned, 'rep', axis=1, tiled=True)]
    ppermute x0 -> x7, waiting for transfers between devices: none -> 8.66 us  [the longest x4 8.65 us: collect(): lower.append(lax.ppermute(lower[-1] if lower else value, axis, pairs))]
  transfers between devices with their start and end apart: 4 -> 11, of which waited for: 4 -> 8; matrix products, arithmetic and copies ran while one was open for 1% -> 1% of each run, Pallas kernels for 0% -> 0%
where the time goes in v1:
time: 589 us; the launch traced here: 588 us
  blocking collectives  280 us (48%)
  waiting for transfers between devices  238 us (40%)
  starting transfers between devices  28.8 us (5%)
  local copies, waits for them, and re-layouts  17.3 us (3%)
  between operations  14.2 us (2%)
  other arithmetic  6.71 us (1%)
    psum x1, blocking collectives, on_device(): weight_grad, bias_grad = lax.psum((weight_term, bias_term), 'row')  280 us
    all_gather x1, waiting for transfers between devices, on_device(): table = lax.all_gather(wide_own, 'row', axis=0, tiled=True)  136 us
    psum x1, waiting for transfers between devices, on_device(): agg = lax.psum(partial_agg.astype(jnp.bfloat16), 'rep')  66.4 us
    all_to_all x1, starting transfers between devices, on_device(): lax.all_to_all(send_pos, 'row', split_axis=0, concat_axis=0, tiled=True)  18.6 us
    all_to_all x1, waiting for transfers between devices, on_device(): lax.all_to_all(send_rows, 'row', split_axis=0, concat_axis=0, tiled=True)  13.9 us
    all_to_all x1, waiting for transfers between devices, on_device(): lax.all_to_all(send_pos, 'row', split_axis=0, concat_axis=0, tiled=True)  12.5 us
  transfers between devices with their start and end apart: 11, of which 8 were waited for; matrix products, arithmetic and copies ran while one was open for 1% of the time, Pallas kernels for 0%

profile of v1, /device:TPU:8, one launch (start us, length us, event | category | flops | bytes accessed | tf_op | source)
XLA Modules:
  0.0 588.3 jit_solution(14362353342627015613)
XLA Ops:
  7.9 3.2 sort.17
  11.1 2.0 gather_fusion
  13.9 18.6 %all-to-all-start = ((s32[64,1,4]{2,1,0:T(1,128)}), s32[64,1,4]{2,1,0:T(1,128)S(1)}, u32[]{:S(2)}, u32[]{:S(2)}) async-start(s32[64,1,4]{2,1,0:T(1,128)} %bitcast), calls=%async_computation | async-start | bytes 65536 | tf_op jit(solution)/shard_map/all_to_all | solution.py:50
  33.2 1.5 gather_fusion.1
  34.7 12.5 %all-to-all-done = s32[64,1,4]{2,1,0:T(1,128)S(1)} async-done(((s32[64,1,4]{2,1,0:T(1,128)}), s32[64,1,4]{2,1,0:T(1,128)S(1)}, u32[]{:S(2)}, u32[]{:S(2)}) %all-to-all-start) | async-done | bytes 1056 | tf_op jit(solution)/shard_map/all_to_all | solution.py:50
  47.2 4.6 all-to-all-start.1
  53.2 13.9 %all-to-all-done.1 = bf16[64,4,16]{2,1,0:T(4,128)(2,1)S(1)} async-done(((bf16[64,4,16]{2,1,0:T(4,128)(2,1)}), bf16[64,4,16]{2,1,0:T(4,128)(2,1)S(1)}, u32[]{:S(2)}, u32[]{:S(2)}) %all-to-all-start.1) | async-done | bytes 8224 | tf_op jit(solution)/shard_map/all_to_all | solution.py:49
  67.1 1.2 scatter_custom_fusion
  68.3 1.7 collective-permute-start.4
  70.0 1.9 collective-permute-done
  72.0 1.7 collective-permute-start.5
  73.7 1.9 collective-permute-done.1
  75.7 2.0 collective-permute-start.6
  77.7 1.6 collective-permute-done.2
  79.9 3.1 collective-permute-done.3
  83.2 1.2 gather_fusion.2
  86.0 136.0 %all-gather.2.cloned.1.call-done = bf16[16384,128]{0,1:T(8,128)(2,1)} async-done(((bf16[256,128]{0,1:T(8,128)(2,1)}), bf16[16384,128]{0,1:T(8,128)(2,1)}) %all-gather.2.cloned.1.call-update) | async-done | bytes 4194320 | tf_op jit(solution)/shard_map/all_gather | solution.py:58
  222.0 6.4 %copy.30 = bf16[16384,128]{1,0:T(8,128)(2,1)} copy(bf16[16384,128]{0,1:T(8,128)(2,1)} %all-gather.2.cloned.1.call-done) | data formatting | bytes 8388608 | tf_op jit(solution)/shard_map/all_gather | solution.py:58
  228.4 2.8 gather_fusion.3
  231.2 1.0 fusion
  232.2 66.4 %all-reduce.3.cloned.1.call-done = bf16[256,128]{1,0:T(8,128)(2,1)} async-done(((bf16[256,128]{1,0:T(8,128)(2,1)}), bf16[256,128]{1,0:T(8,128)(2,1)}) %all-reduce.3.cloned.1.call-update) | async-done | bytes 65552 | tf_op jit(solution)/shard_map/psum | solution.py:63
  298.7 1.7 convert_reduce_fusion
  300.4 1.0 fusion.10
  301.4 280.1 %all-reduce = (f32[128,32]{0,1:T(8,128)}, f32[32]{0:T(128)}) all-reduce(f32[128,32]{0,1:T(8,128)S(1)} %fusion.10, f32[32]{0:T(128)S(1)} %get-tuple-element.7), channel_id=1, replica_groups=mesh['row'=64,'rep'=8] {'row'}, use_global_device_ids=true, to_apply=%region_3.4 | all-reduce | flops 4128 | bytes 33024 | tf_op jit(solution)/shard_map/psum | solution.py:70
  (52 shorter events, 6.0 us)
Async XLA Ops:
  7.2 224.1 %copy-start = (bf16[2,8,128,128]{3,2,1,0:T(8,128)(2,1)S(1)}, bf16[2,8,128,128]{3,2,1,0:T(8,128)(2,1)}, u32[]{:S(2)}) copy-start(bf16[2,8,128,128]{3,2,1,0:T(8,128)(2,1)} %param.12) | copy-start | bytes 1572868
  13.9 33.3 %all-to-all-start = ((s32[64,1,4]{2,1,0:T(1,128)}), s32[64,1,4]{2,1,0:T(1,128)S(1)}, u32[]{:S(2)}, u32[]{:S(2)}) async-start(s32[64,1,4]{2,1,0:T(1,128)} %bitcast), calls=%async_computation | async-start | bytes 65536 | tf_op jit(solution)/shard_map/all_to_all | solution.py:50
  47.2 19.9 %all-to-all-start.1 = ((bf16[64,4,16]{2,1,0:T(4,128)(2,1)}), bf16[64,4,16]{2,1,0:T(4,128)(2,1)S(1)}, u32[]{:S(2)}, u32[]{:S(2)}) async-start(bf16[64,4,16]{2,1,0:T(4,128)(2,1)} %bitcast.2), calls=%async_computation.1 | async-start | bytes 131072 | tf_op jit(solution)/shard_map/all_to_all | solution.py:49
  51.8 170.2 %all-gather.2.cloned.1.call-start = ((), (), s32[]{:S(2)}) async-start(), calls=%async_computation.2 | async-start | bytes 4259840 | tf_op jit(solution)/shard_map/all_gather | solution.py:58
  68.3 3.7 collective-permute-start
  68.3 3.7 collective-permute-start.4
  72.0 3.7 collective-permute-start.1
  72.0 3.7 collective-permute-start.5
  75.7 3.7 collective-permute-start.2
  75.7 4.2 collective-permute-start.6
  79.4 3.7 collective-permute-start.3
  84.4 214.3 %all-reduce.3.cloned.1.call-start = ((), (), s32[]{:S(2)}) async-start(), calls=%async_computation.3 | async-start | bytes 131072 | tf_op jit(solution)/shard_map/psum | solution.py:63
  85.9 212.7 %copy-start.1 = (bf16[256,32]{0,1:T(8,128)(2,1)S(1)}, bf16[256,32]{0,1:T(8,128)(2,1)}, u32[]{:S(2)}) copy-start(bf16[256,32]{0,1:T(8,128)(2,1)} %param.15) | copy-start | bytes 49156
  85.9 212.7 %copy-start.2 = (bf16[128,32]{0,1:T(8,128)(2,1)S(1)}, bf16[128,32]{0,1:T(8,128)(2,1)}, u32[]{:S(2)}) copy-start(bf16[128,32]{0,1:T(8,128)(2,1)} %param.13) | copy-start | bytes 24580
  85.9 212.7 %copy-start.3 = (f32[32]{0:T(128)S(1)}, f32[32]{0:T(128)}, u32[]{:S(2)}) copy-start(f32[32]{0:T(128)} %param.14) | copy-start | bytes 388
Sparse Core Ops, SparseCore 0:
  84.5 137.4 all-gather.1
  232.4 66.2 all-reduce.2

commit v2 on v0

--- a/solution.py
+++ b/solution.py
@@ -38,7 +38,7 @@
     slot_ids = lax.axis_index("rep") * slots_dev + jnp.arange(slots_dev, dtype=jnp.int32)
     live = slot_ids[None, :] < block_count[:, None]
     partial_agg = block_product(tiles, block_cols, live, table, rows_part)
-    agg = lax.psum(partial_agg.astype(jnp.bfloat16), "rep")
+    agg = jnp.sum(lax.all_gather(partial_agg.astype(jnp.bfloat16), "rep"), axis=0)
     pre = jnp.dot(agg, weight, preferred_element_type=jnp.float32) + bias
     hidden = jax.nn.silu(pre).astype(jnp.bfloat16)
     sig = jax.nn.sigmoid(pre)

time: 584 us -> 525 us (0.90)
  waiting for transfers between devices: 226 us -> 160 us
  blocking collectives: 294 us -> 303 us
    psum x1 -> x0, waiting for transfers between devices: 66.4 us -> none  [on_device(): agg = lax.psum(partial_agg.astype(jnp.bfloat16), 'rep')]
    all_gather x0 -> x1, blocking collectives: none -> 13.2 us  [on_device(): lax.all_gather(partial_agg.astype(jnp.bfloat16), 'rep')]
  transfers between devices with their start and end apart: 4 -> 3, of which waited for: 4 -> 3; matrix products, arithmetic and copies ran while one was open for 1% -> 1% of each run, Pallas kernels for 0% -> 0%
where the time goes in v2:
time: 525 us; the launch traced here: 524 us
  blocking collectives  303 us (58%)
  waiting for transfers between devices  160 us (30%)
  starting transfers between devices  23.2 us (4%)
  local copies, waits for them, and re-layouts  15.5 us (3%)
  between operations  14.2 us (3%)
  other arithmetic  6.77 us (1%)
    psum x1, blocking collectives, on_device(): weight_grad, bias_grad = lax.psum((weight_term, bias_term), 'row')  276 us
    all_gather x1, waiting for transfers between devices, on_device(): table = lax.all_gather(wide_own, 'row', axis=0, tiled=True)  133 us
    all_to_all x1, starting transfers between devices, on_device(): lax.all_to_all(send_pos, 'row', split_axis=0, concat_axis=0, tiled=True)  18.6 us
    all_gather x1, blocking collectives, on_device(): wide_own = lax.all_gather(owned, 'rep', axis=1, tiled=True)  14 us
    all_to_all x1, waiting for transfers between devices, on_device(): lax.all_to_all(send_rows, 'row', split_axis=0, concat_axis=0, tiled=True)  13.9 us
    all_gather x1, blocking collectives, on_device(): lax.all_gather(partial_agg.astype(jnp.bfloat16), 'rep')  13.2 us
    all_to_all x1, waiting for transfers between devices, on_device(): lax.all_to_all(send_pos, 'row', split_axis=0, concat_axis=0, tiled=True)  12.5 us
  transfers between devices with their start and end apart: 3, of which 3 were waited for; matrix products, arithmetic and copies ran while one was open for 1% of the time, Pallas kernels for 0%

profile of v2, /device:TPU:8, one launch (start us, length us, event | category | flops | bytes accessed | tf_op | source)
XLA Modules:
  0.0 524.3 jit_solution(3482279730385450446)
XLA Ops:
  7.2 0.7 and_select_fusion
  7.9 3.2 sort.17
  11.1 2.0 gather_fusion
  13.2 0.6 add_select_fusion
  13.8 18.6 %all-to-all-start = ((s32[64,1,4]{2,1,0:T(1,128)}), s32[64,1,4]{2,1,0:T(1,128)S(1)}, u32[]{:S(2)}, u32[]{:S(2)}) async-start(s32[64,1,4]{2,1,0:T(1,128)} %bitcast), calls=%async_computation | async-start | bytes 65536 | tf_op jit(solution)/shard_map/all_to_all | solution.py:28
  32.4 0.8 copy.18
  33.2 1.5 gather_fusion.1
  34.7 12.5 %all-to-all-done = s32[64,1,4]{2,1,0:T(1,128)S(1)} async-done(((s32[64,1,4]{2,1,0:T(1,128)}), s32[64,1,4]{2,1,0:T(1,128)S(1)}, u32[]{:S(2)}, u32[]{:S(2)}) %all-to-all-start) | async-done | bytes 1056 | tf_op jit(solution)/shard_map/all_to_all | solution.py:28
  47.2 4.6 all-to-all-start.1
  51.8 0.5 broadcast.122
  52.3 0.7 reduce.4
  53.2 13.9 %all-to-all-done.1 = bf16[64,4,16]{2,1,0:T(4,128)(2,1)S(1)} async-done(((bf16[64,4,16]{2,1,0:T(4,128)(2,1)}), bf16[64,4,16]{2,1,0:T(4,128)(2,1)S(1)}, u32[]{:S(2)}, u32[]{:S(2)}) %all-to-all-start.1) | async-done | bytes 8224 | tf_op jit(solution)/shard_map/all_to_all | solution.py:27
  67.1 1.2 scatter_custom_fusion
  68.3 14.0 %all_gather.10 = bf16[256,128]{0,1:T(8,128)(2,1)} all-gather(bf16[256,16]{0,1:T(8,128)(2,1)S(1)} %copy.19), channel_id=1, replica_groups=mesh['row'=64,'rep'=8] {'rep'}, dimensions={1}, use_global_device_ids=true | all-gather | bytes 73728 | tf_op jit(solution)/shard_map/all_gather | solution.py:35
  82.4 0.7 compare_select_fusion.1
  83.2 0.7 broadcast_compare_fusion
  83.9 133.5 %all-gather.2.cloned.1.call-done = bf16[16384,128]{0,1:T(8,128)(2,1)} async-done(((bf16[256,128]{0,1:T(8,128)(2,1)}), bf16[16384,128]{0,1:T(8,128)(2,1)}) %all-gather.2.cloned.1.call-update) | async-done | bytes 4194320 | tf_op jit(solution)/shard_map/all_gather | solution.py:36
  217.4 6.4 %copy.20 = bf16[16384,128]{1,0:T(8,128)(2,1)} copy(bf16[16384,128]{0,1:T(8,128)(2,1)} %all-gather.2.cloned.1.call-done) | data formatting | bytes 8388608 | tf_op jit(solution)/shard_map/all_gather | solution.py:36
  223.7 2.8 gather_fusion.2
  226.6 0.4 fusion
  226.9 13.2 %all_gather.12 = bf16[8,256,128]{2,1,0:T(8,128)(2,1)S(1)} all-gather(bf16[1,256,128]{2,1,0:T(8,128)(2,1)S(1)} %bitcast.21), channel_id=1, replica_groups=mesh['row'=64,'rep'=8] {'rep'}, dimensions={0}, use_global_device_ids=true | all-gather | bytes 589824 | tf_op jit(solution)/shard_map/all_gather | solution.py:41
  240.2 0.9 convert_reduce_fusion
  241.1 0.1 fusion.8
  241.2 276.2 %all-reduce = (f32[128,32]{0,1:T(8,128)}, f32[32]{0:T(128)}) all-reduce(f32[128,32]{0,1:T(8,128)S(1)} %fusion.8, f32[32]{0:T(128)S(1)} %get-tuple-element.7), channel_id=1, replica_groups=mesh['row'=64,'rep'=8] {'row'}, use_global_device_ids=true, to_apply=%region_3.4 | all-reduce | flops 4128 | bytes 33024 | tf_op jit(solution)/shard_map/psum | solution.py:48
  (21 shorter events, 0.5 us)
Async XLA Ops:
  7.2 219.4 %copy-start = (bf16[2,8,128,128]{3,2,1,0:T(8,128)(2,1)S(1)}, bf16[2,8,128,128]{3,2,1,0:T(8,128)(2,1)}, u32[]{:S(2)}) copy-start(bf16[2,8,128,128]{3,2,1,0:T(8,128)(2,1)} %param.12) | copy-start | bytes 1572868
  13.8 33.3 %all-to-all-start = ((s32[64,1,4]{2,1,0:T(1,128)}), s32[64,1,4]{2,1,0:T(1,128)S(1)}, u32[]{:S(2)}, u32[]{:S(2)}) async-start(s32[64,1,4]{2,1,0:T(1,128)} %bitcast), calls=%async_computation | async-start | bytes 65536 | tf_op jit(solution)/shard_map/all_to_all | solution.py:28
  47.2 19.9 %all-to-all-start.1 = ((bf16[64,4,16]{2,1,0:T(4,128)(2,1)}), bf16[64,4,16]{2,1,0:T(4,128)(2,1)S(1)}, u32[]{:S(2)}, u32[]{:S(2)}) async-start(bf16[64,4,16]{2,1,0:T(4,128)(2,1)} %bitcast.2), calls=%async_computation.1 | async-start | bytes 131072 | tf_op jit(solution)/shard_map/all_to_all | solution.py:27
  51.8 165.6 %all-gather.2.cloned.1.call-start = ((), (), s32[]{:S(2)}) async-start(), calls=%async_computation.2 | async-start | bytes 4259840 | tf_op jit(solution)/shard_map/all_gather | solution.py:36
  83.9 156.3 %copy-start.1 = (bf16[256,32]{0,1:T(8,128)(2,1)S(1)}, bf16[256,32]{0,1:T(8,128)(2,1)}, u32[]{:S(2)}) copy-start(bf16[256,32]{0,1:T(8,128)(2,1)} %param.15) | copy-start | bytes 49156
  83.9 156.3 %copy-start.2 = (bf16[128,32]{0,1:T(8,128)(2,1)S(1)}, bf16[128,32]{0,1:T(8,128)(2,1)}, u32[]{:S(2)}) copy-start(bf16[128,32]{0,1:T(8,128)(2,1)} %param.13) | copy-start | bytes 24580
  83.9 156.3 %copy-start.3 = (f32[32]{0:T(128)S(1)}, f32[32]{0:T(128)}, u32[]{:S(2)}) copy-start(f32[32]{0:T(128)} %param.14) | copy-start | bytes 388
Sparse Core Ops, SparseCore 0:
  82.5 134.8 all-gather.1
